TPU v7x, 32 devices: a whole 2x2x4 slice. The times are simulated.
32 devices in a mesh: ind: 8 (over z, x), var: 4 (over y, core).
Axes of the slice: x: 2, y: 2, z: 4, core: 2. Of those that a mesh axis runs over, the one named last changes fastest.
Arguments:
- genotypes: float32 [256, 16384], P('var', 'ind'), may hold values from -30 to 30
- variance_comp: float32 [2], replicated, may hold values from 0.5 to 1.5
- grm_tiles: bfloat16 [80, 512, 512], P('ind'), may hold values from -1 to 6, as said below
- tile_rows: int32 [80], P('ind'), may hold values from 0 to 3, as said below
- tile_cols: int32 [80], P('ind'), may hold values from 0 to 31, as said below
- tile_live: int32 [8], P('ind'), may hold values from 5 to 10, as said below
Outputs:
- solution: float32 [256, 16384], P('var', 'ind')
- gene_gram: float32 [256, 4], P('var')
Inputs may be any that keep to these rules, and one draw needn't show every extreme that they name: `grm_tiles`: every diagonal tile is symmetric, and the tiles of two live slots that form a transposed pair are transposes of each other, so K is symmetric. Slots r < 4 of each index i of ind hold its diagonal tiles: tile_rows = r and tile_cols = i * 4 + r. `tile_cols`: every other slot of index i names a column tile j * 4 + ((i + t) mod 4) of another index j != i, with t < 2. Live off slots come in transposed pairs: a live slot of i at row tile r naming column tile j * 4 + u goes with a live slot of j at row tile u naming column tile i * 4 + r. Some index uses 2 distinct column tiles of one other index. `tile_live`: some index of ind uses all 10 slots.
All inputs are finite; a program needn't handle non-finite values.
Results may differ from a plain program's by a relative error of at most 0.0003.
Values sent between devices are 32-bit elements; how exact they have to be, the bound alone decides.
No kernel may reach another device: no remote copies, remote signals or barrier semaphores. Data moves between devices by JAX's collectives and lax.ppermute only.
A program may use at most 192 MiB of HBM per device.

v0:
```python
import jax
import jax.numpy as jnp
from jax import lax
from jax.sharding import PartitionSpec as P

VARS_GENE = 4
GENES = 64
ITERS = 2
NEED = 2


def local(genotypes, variance_comp, grm_tiles, tile_rows, tile_cols, tile_live):
    cols_here, rows_here = genotypes.shape
    tile_size = grm_tiles.shape[1]
    slot_count = grm_tiles.shape[0]
    row_tiles = rows_here // tile_size
    my_index = lax.axis_index("ind")
    peer_count = lax.axis_size("ind")
    tau_noise = variance_comp[0]
    tau_kin = variance_comp[1]
    live_count = tile_live[0]
    diag_tiles = grm_tiles[:row_tiles]
    off_tiles = grm_tiles[row_tiles:]
    diag_values = jnp.diagonal(diag_tiles, axis1=1, axis2=2).astype(jnp.float32).reshape(rows_here)
    precond = tau_noise + tau_kin * diag_values
    off_rows = tile_rows[row_tiles:]
    off_cols = tile_cols[row_tiles:]
    live_mask = (jnp.arange(row_tiles, slot_count, dtype=jnp.int32) < live_count).astype(
        jnp.float32
    )
    onehot = (off_rows[:, None] == jnp.arange(row_tiles, dtype=jnp.int32)[None, :]).astype(
        jnp.float32
    )
    onehot = onehot * live_mask[:, None]
    solution = jnp.zeros_like(genotypes)
    resid = genotypes
    scaled = resid / precond[None, :]
    direction = scaled
    rz_now = lax.psum(jnp.sum(resid * scaled, axis=1), "ind")
    for rounds in range(ITERS):
        pieces = direction.reshape(cols_here, row_tiles, tile_size)
        table = (
            jnp.arange(peer_count, dtype=jnp.int32)[:, None]
            + jnp.arange(NEED, dtype=jnp.int32)[None, :]
        ) % row_tiles
        outgoing = pieces[:, table]
        arrived = lax.all_to_all(outgoing, "ind", split_axis=1, concat_axis=1, tiled=True)
        flat = arrived.reshape(cols_here, peer_count * NEED, tile_size)
        position = off_cols // row_tiles * NEED + (off_cols % row_tiles - my_index) % row_tiles
        position = jnp.clip(position, 0, peer_count * NEED - 1)
        picked = jnp.take(flat, position, axis=1)
        apply_pieces = direction.reshape(cols_here, row_tiles, tile_size)
        near = jnp.einsum(
            "crk,rqk->crq",
            apply_pieces,
            diag_tiles,
            precision=lax.Precision.HIGHEST,
            preferred_element_type=jnp.float32,
        )
        far = jnp.einsum(
            "csk,sqk->csq",
            picked,
            off_tiles,
            precision=lax.Precision.HIGHEST,
            preferred_element_type=jnp.float32,
        )
        far = jnp.einsum("csq,sr->crq", far, onehot, precision=lax.Precision.HIGHEST)
        image = tau_noise * direction + tau_kin * (near + far).reshape(cols_here, rows_here)
        alpha = rz_now / lax.psum(jnp.sum(direction * image, axis=1), "ind")
        solution = solution + alpha[:, None] * direction
        resid = resid - alpha[:, None] * image
        if rounds + 1 < ITERS:
            scaled = resid / precond[None, :]
            rz_next = lax.psum(jnp.sum(resid * scaled, axis=1), "ind")
            direction = scaled + (rz_next / rz_now)[:, None] * direction
            rz_now = rz_next
    var_index = lax.axis_index("var")
    gathered = lax.all_gather(solution, "var", axis=0, tiled=True)
    split_cols = gathered.reshape(VARS_GENE, GENES, rows_here)
    first_gene = var_index * cols_here % GENES
    matching = lax.dynamic_slice_in_dim(split_cols, first_gene, cols_here, 1)
    partial_gram = jnp.einsum("jn,bjn->jb", genotypes, matching, precision=lax.Precision.HIGHEST)
    total_gram = lax.psum(partial_gram, "ind")
    gene_gram = total_gram / (peer_count * rows_here)
    return (solution, gene_gram)


def solution(mesh):
    placed = (P("var", "ind"), P(), P("ind", None, None), P("ind"), P("ind"), P("ind"))
    return jax.shard_map(
        local,
        mesh=mesh,
        in_specs=placed,
        out_specs=(P("var", "ind"), P("var", None)),
        check_vma=False,
    )
```

profile of v0, /device:TPU:0, one launch (start us, length us, event | category | flops | bytes accessed | tf_op | source)
XLA Modules:
  0.0 310.4 jit_solution(10890623376764823809)
XLA Ops:
  7.2 1.6 slice-done
  8.8 41.5 %copy.31 = bf16[4,512,512]{0,2,1:T(8,128)(2,1)} copy(bf16[4,512,512]{2,1,0:T(8,128)(2,1)S(1)} %slice-done) | data formatting | bytes 4194304 | tf_op jit(solution)/shard_map/slice | solution.py:22
  50.9 6.5 %gather_fusion = bf16[512,4]{1,0:T(8,128)(2,1)S(1)} fusion(bf16[4,512,512]{0,2,1:T(8,128)(2,1)} %copy.31, s32[512]{0:T(512)S(1)} %bitcast.54), kind=kCustom, calls=%fused_computation.2 | custom fusion | bytes 12288 | tf_op jit(solution)/shard_map/jit(diagonal)/gather | solution.py:24
  57.4 1.3 multiply_add_fusion.3
  59.0 2.0 gather_fusion.1
  61.1 7.4 %all-to-all-start = ((f32[64,8,2,512]{3,0,2,1:T(8,128)}), f32[64,8,2,512]{3,0,2,1:T(8,128)S(1)}, u32[]{:S(2)}, u32[]{:S(2)}) async-start(f32[64,8,2,512]{3,0,2,1:T(8,128)} %bitcast.60), calls=%async_computation | async-start | bytes 4194304 | tf_op jit(solution)/shard_map/all_to_all | solution.py:47
  69.4 47.3 %all-to-all-done = f32[64,8,2,512]{3,0,2,1:T(8,128)S(1)} async-done(((f32[64,8,2,512]{3,0,2,1:T(8,128)}), f32[64,8,2,512]{3,0,2,1:T(8,128)S(1)}, u32[]{:S(2)}, u32[]{:S(2)}) %all-to-all-start) | async-done | bytes 2097184 | tf_op jit(solution)/shard_map/all_to_all | solution.py:47
  116.7 1.5 gather_fusion.3
  118.2 5.1 %fusion.6 = f32[64,6,512]{2,0,1:T(8,128)S(1)} fusion(bf16[10,512,512]{2,1,0:T(8,128)(2,1)} %param.10, f32[6,64,512]{2,1,0:T(8,128)} %gather_fusion.3, pred[6]{0:T(512)(128)(4,1)S(1)} %get-tuple-element.7), kind=kOutput, calls=%fused_computation.11 | convolution fusion | flops 1208156160 | bytes 4718598 | tf_op jit(solution)/shard_map/csk,sqk->csq/dot_general | solution.py:60
  123.3 1.4 fusion.18
  124.7 4.3 %fusion.15 = f32[4,8,8,512]{3,2,1,0:T(8,128)S(1)} fusion(f32[4,64,512]{2,0,1:T(4,128)S(1)} %fusion.18, f32[]{:T(128)} %bitcast.1, f32[8,4,8,512]{3,2,1,0:T(8,128)S(1)} %bitcast.68, bf16[10,512,512]{2,1,0:T(8,128)(2,1)} %param.10), kind=kOutput, calls=%fused_computation.18 | convolution fusion | flops 805568512 | bytes 3670528 | tf_op jit(solution)/shard_map/crk,rqk->crq/dot_general | solution.py:53
  129.9 19.5 %all-reduce = (f32[64]{0:T(128)S(1)}, f32[64]{0:T(128)S(1)}) all-reduce(f32[64]{0:T(128)S(1)} %get-tuple-element.4, f32[64]{0:T(128)S(1)} %get-tuple-element.3), channel_id=1, replica_groups=mesh['ind'=8,'var'=4] {'ind'}, use_global_device_ids=true, to_apply=%region_1.2 | all-reduce | flops 128 | bytes 1024 | tf_op jit(solution)/shard_map/psum | solution.py:39
  149.4 0.9 multiply_reduce_fusion.1
  150.3 17.1 %psum.37 = f32[64]{0:T(128)S(1)} all-reduce(f32[64]{0:T(128)S(1)} %multiply_reduce_fusion.1), channel_id=1, replica_groups=mesh['ind'=8,'var'=4] {'ind'}, use_global_device_ids=true, to_apply=%region_5.7 | all-reduce | flops 64 | bytes 512 | tf_op jit(solution)/shard_map/psum | solution.py:74
  168.4 2.0 gather_fusion.2
  170.4 45.8 %all_to_all.10 = f32[64,8,2,512]{3,0,2,1:T(8,128)} all-to-all(f32[64,8,2,512]{3,0,2,1:T(8,128)} %bitcast.61), channel_id=1, replica_groups=mesh['ind'=8,'var'=4] {'ind'}, dimensions={1} | all-to-all | bytes 4194304 | tf_op jit(solution)/shard_map/all_to_all | solution.py:47
  216.2 2.2 gather_fusion.4
  218.4 4.9 %fusion.9 = f32[64,6,512]{2,0,1:T(8,128)S(1)} fusion(bf16[10,512,512]{2,1,0:T(8,128)(2,1)} %param.10, f32[6,64,512]{2,1,0:T(8,128)S(1)} %gather_fusion.4, pred[6]{0:T(512)(128)(4,1)S(1)} %get-tuple-element.7), kind=kOutput, calls=%fused_computation.12 | convolution fusion | flops 1208156160 | bytes 4718598 | tf_op jit(solution)/shard_map/csk,sqk->csq/dot_general | solution.py:60
  223.3 1.4 fusion.16
  224.7 4.3 %fusion.13 = f32[4,8,8,512]{3,2,1,0:T(8,128)S(1)} fusion(f32[4,64,512]{2,0,1:T(4,128)S(1)} %fusion.16, f32[]{:T(128)} %bitcast.1, f32[8,4,8,512]{3,2,1,0:T(8,128)S(1)} %bitcast.57, bf16[10,512,512]{2,1,0:T(8,128)(2,1)} %param.10), kind=kOutput, calls=%fused_computation.15 | convolution fusion | flops 805568512 | bytes 3670528 | tf_op jit(solution)/shard_map/crk,rqk->crq/dot_general | solution.py:53
  229.8 19.4 %psum.38 = f32[64]{0:T(128)S(1)} all-reduce(f32[64]{0:T(128)S(1)} %multiply_reduce_fusion), channel_id=1, replica_groups=mesh['ind'=8,'var'=4] {'ind'}, use_global_device_ids=true, to_apply=%region_7.9 | all-reduce | flops 64 | bytes 512 | tf_op jit(solution)/shard_map/psum | solution.py:69
  250.2 20.1 %all-gather.2.cloned.1.call-done = f32[256,2048]{1,0:T(8,128)} async-done(((f32[64,2048]{1,0:T(8,128)}), f32[256,2048]{1,0:T(8,128)}) %all-gather.2.cloned.1.call-update) | async-done | bytes 2097168 | tf_op jit(solution)/shard_map/all_gather | solution.py:78
  270.3 11.3 %fusion.4 = f32[64,1,4]{2,1,0:T(1,128)S(1)} fusion(f32[4,64,2048]{2,1,0:T(8,128)} %bitcast.77, f32[64,2048,1]{1,0,2:T(8,128)S(1)} %bitcast.55), kind=kOutput, calls=%fused_computation.9 | convolution fusion | flops 6291456 | bytes 2622464 | tf_op jit(solution)/shard_map/jn,bjn->jb/dot_general | solution.py:82
  281.6 21.4 %psum.39 = f32[64,4]{0,1:T(4,128)S(1)} all-reduce(f32[64,4]{0,1:T(4,128)S(1)} %bitcast.76), channel_id=1, replica_groups=mesh['ind'=8,'var'=4] {'ind'}, use_global_device_ids=true, to_apply=%region_8.10 | all-reduce | flops 256 | bytes 2048 | tf_op jit(solution)/shard_map/psum | solution.py:83
  (36 shorter events, 5.4 us)
Async XLA Ops:
  7.2 1.6 slice-start
  8.8 41.5 %copy-start.1 = (f32[2]{0:T(128)S(1)}, f32[2]{0:T(128)}, u32[]{:S(2)}) copy-start(f32[2]{0:T(128)} %param.9) | copy-start | bytes 28
  8.8 50.0 %copy-start = (f32[64,2048]{1,0:T(8,128)S(1)}, f32[64,2048]{1,0:T(8,128)}, u32[]{:S(2)}) copy-start(f32[64,2048]{1,0:T(8,128)} %param.8) | copy-start | bytes 1572868
  61.1 8.1 %copy-start.3 = (s32[10]{0:T(128)S(1)}, s32[10]{0:T(128)}, u32[]{:S(2)}) copy-start(s32[10]{0:T(128)} %param.11) | copy-start | bytes 124
  61.1 8.2 %copy-start.2 = (s32[10]{0:T(128)S(1)}, s32[10]{0:T(128)}, u32[]{:S(2)}) copy-start(s32[10]{0:T(128)} %param.12) | copy-start | bytes 124
  61.1 55.7 %all-to-all-start = ((f32[64,8,2,512]{3,0,2,1:T(8,128)}), f32[64,8,2,512]{3,0,2,1:T(8,128)S(1)}, u32[]{:S(2)}, u32[]{:S(2)}) async-start(f32[64,8,2,512]{3,0,2,1:T(8,128)} %bitcast.60), calls=%async_computation | async-start | bytes 4194304 | tf_op jit(solution)/shard_map/all_to_all | solution.py:47
  68.5 201.8 %all-gather.2.cloned.1.call-start = ((), (), s32[]{:S(2)}) async-start(), calls=%async_computation.2 | async-start | bytes 2621440 | tf_op jit(solution)/shard_map/all_gather | solution.py:78
Sparse Core Ops, SparseCore 0:
  250.3 19.8 all-gather.1
where the time goes:
time: 311 us; the launch traced here: 310 us
  blocking collectives  123 us (40%)
  waiting for transfers between devices  67.4 us (22%)
  local copies, waits for them, and re-layouts  58.4 us (19%)
  matrix products  32.6 us (10%)
  between operations  14.8 us (5%)
  starting transfers between devices  7.45 us (2%)
  other arithmetic  6.54 us (2%)
    all_to_all x1, waiting for transfers between devices, local(): lax.all_to_all(outgoing, 'ind', split_axis=1, concat_axis=1, tiled=True)  47.3 us
    all_to_all x1, blocking collectives, local(): lax.all_to_all(outgoing, 'ind', split_axis=1, concat_axis=1, tiled=True)  45.8 us
    slice x3, local copies, waits for them, and re-layouts, local(): diag_tiles = grm_tiles[:row_tiles]  43.1 us
    psum x1, blocking collectives, local(): total_gram = lax.psum(partial_gram, 'ind')  21.4 us
    all_gather x1, waiting for transfers between devices, local(): gathered = lax.all_gather(solution, 'var', axis=0, tiled=True)  20.1 us
    psum x1, blocking collectives, local(): rz_now = lax.psum(jnp.sum(resid * scaled, axis=1), 'ind')  19.5 us
    psum x1, blocking collectives, local(): alpha = rz_now / lax.psum(jnp.sum(direction * image, axis=1), 'ind')  19.4 us
    psum x1, blocking collectives, local(): rz_next = lax.psum(jnp.sum(resid * scaled, axis=1), 'ind')  17.1 us
  transfers between devices with their start and end apart: 2, of which 2 were waited for; matrix products, arithmetic and copies ran while one was open for 0% of the time, Pallas kernels for 0%

commit v1 on v0

--- a/solution.py
+++ b/solution.py
@@ -7,6 +7,27 @@
 GENES = 64
 ITERS = 2
 NEED = 2
+
+
+def start_rails(block_in, axis_k):
+    block_in = jnp.moveaxis(block_in, 0, axis_k)
+    tall = block_in.shape
+    return block_in.reshape(*tall[:axis_k], tall[axis_k] * tall[axis_k + 1], *tall[axis_k + 2 :])
+
+
+def watch_the_layers_all(s0, mesh_name):
+    far_arr = s0[None]
+    lanes = lax.psum(1, mesh_name)
+    for idx in range(lanes.bit_length() - 1):
+        b_now = 1 << idx
+        stack_in = []
+        for it in [*range(lanes)]:
+            stack_in.append((it, it ^ b_now))
+        right_arr = lax.ppermute(far_arr, mesh_name, stack_in)
+        known = jnp.stack([far_arr, right_arr], 0)
+        answer = lax.axis_index(mesh_name) >> idx & 1
+        far_arr = jnp.where(answer == 0, known, known[::-1]).reshape(-1, *s0.shape)
+    return far_arr
 
 
 def local(genotypes, variance_comp, grm_tiles, tile_rows, tile_cols, tile_live):
@@ -75,7 +96,7 @@
             direction = scaled + (rz_next / rz_now)[:, None] * direction
             rz_now = rz_next
     var_index = lax.axis_index("var")
-    gathered = lax.all_gather(solution, "var", axis=0, tiled=True)
+    gathered = start_rails(watch_the_layers_all(solution, "var"), 0)
     split_cols = gathered.reshape(VARS_GENE, GENES, rows_here)
     first_gene = var_index * cols_here % GENES
     matching = lax.dynamic_slice_in_dim(split_cols, first_gene, cols_here, 1)

time: 311 us -> 300 us (0.965)
  between operations: 14.8 us -> 1.48 us
  waiting for transfers between devices: 67.4 us -> 73.1 us
  blocking collectives: 123 us -> 119 us
    ppermute x0 -> x2, waiting for transfers between devices: none -> 25.7 us  [watch_the_layers_all(): right_arr = lax.ppermute(far_arr, mesh_name, stack_in)]
    all_gather x1 -> x0, waiting for transfers between devices: 20.1 us -> none  [local(): gathered = lax.all_gather(solution, 'var', axis=0, tiled=True)]
    psum x1, blocking collectives: 21.4 us -> 17.1 us  [local(): total_gram = lax.psum(partial_gram, 'ind')]
  transfers between devices with their start and end apart: 2 -> 3, of which waited for: 2 -> 3; matrix products, arithmetic and copies ran while one was open for 0% -> 0% of each run, Pallas kernels for 0% -> 0%
where the time goes in v1:
time: 300 us
  blocking collectives  119 us (40%)
  waiting for transfers between devices  73.1 us (24%)
  local copies, waits for them, and re-layouts  58.4 us (19%)
  matrix products  31 us (10%)
  starting transfers between devices  9.06 us (3%)
  other arithmetic  7.43 us (2%)
    all_to_all x1, waiting for transfers between devices, local(): lax.all_to_all(outgoing, 'ind', split_axis=1, concat_axis=1, tiled=True)  47.4 us
    all_to_all x1, blocking collectives, local(): lax.all_to_all(outgoing, 'ind', split_axis=1, concat_axis=1, tiled=True)  45.8 us
    slice x3, local copies, waits for them, and re-layouts, local(): diag_tiles = grm_tiles[:row_tiles]  43.1 us
    ppermute x2, waiting for transfers between devices, watch_the_layers_all(): right_arr = lax.ppermute(far_arr, mesh_name, stack_in)  25.7 us
    psum x1, blocking collectives, local(): alpha = rz_now / lax.psum(jnp.sum(direction * image, axis=1), 'ind')  19.6 us
    psum x1, blocking collectives, local(): rz_now = lax.psum(jnp.sum(resid * scaled, axis=1), 'ind')  19.5 us
    psum x1, blocking collectives, local(): total_gram = lax.psum(partial_gram, 'ind')  17.1 us
    psum x1, blocking collectives, local(): rz_next = lax.psum(jnp.sum(resid * scaled, axis=1), 'ind')  17.1 us
  transfers between devices with their start and end apart: 3, of which 3 were waited for; matrix products, arithmetic and copies ran while one was open for 0% of the time, Pallas kernels for 0%

profile of v1, /device:TPU:0, one launch (start us, length us, event | category | flops | bytes accessed | tf_op | source)
XLA Modules:
  0.0 299.7 jit_solution(7843961947087999338)
XLA Ops:
  0.7 1.6 slice-done
  2.3 41.5 %copy.31 = bf16[4,512,512]{0,2,1:T(8,128)(2,1)} copy(bf16[4,512,512]{2,1,0:T(8,128)(2,1)S(1)} %slice-done) | data formatting | bytes 4194304 | tf_op jit(solution)/shard_map/slice | solution.py:43
  44.4 6.5 %gather_fusion = bf16[512,4]{1,0:T(8,128)(2,1)S(1)} fusion(bf16[4,512,512]{0,2,1:T(8,128)(2,1)} %copy.31, s32[512]{0:T(512)S(1)} %bitcast.62), kind=kCustom, calls=%fused_computation.2 | custom fusion | bytes 12288 | tf_op jit(solution)/shard_map/jit(diagonal)/gather | solution.py:45
  52.5 2.0 gather_fusion.1
  54.5 7.4 %all-to-all-start = ((f32[64,8,2,512]{3,0,2,1:T(8,128)}), f32[64,8,2,512]{3,0,2,1:T(8,128)S(1)}, u32[]{:S(2)}, u32[]{:S(2)}) async-start(f32[64,8,2,512]{3,0,2,1:T(8,128)} %bitcast.68), calls=%async_computation | async-start | bytes 4194304 | tf_op jit(solution)/shard_map/all_to_all | solution.py:68
  62.8 47.4 %all-to-all-done = f32[64,8,2,512]{3,0,2,1:T(8,128)S(1)} async-done(((f32[64,8,2,512]{3,0,2,1:T(8,128)}), f32[64,8,2,512]{3,0,2,1:T(8,128)S(1)}, u32[]{:S(2)}, u32[]{:S(2)}) %all-to-all-start) | async-done | bytes 2097184 | tf_op jit(solution)/shard_map/all_to_all | solution.py:68
  110.2 1.5 gather_fusion.3
  111.6 5.1 %fusion.6 = f32[64,6,512]{2,0,1:T(8,128)S(1)} fusion(bf16[10,512,512]{2,1,0:T(8,128)(2,1)} %param.10, f32[6,64,512]{2,1,0:T(8,128)} %gather_fusion.3, pred[6]{0:T(512)(128)(4,1)S(1)} %get-tuple-element.7), kind=kOutput, calls=%fused_computation.14 | convolution fusion | flops 1208156160 | bytes 4718598 | tf_op jit(solution)/shard_map/csk,sqk->csq/dot_general | solution.py:81
  116.8 1.4 fusion.18
  118.2 4.3 %fusion.15 = f32[4,8,8,512]{3,2,1,0:T(8,128)S(1)} fusion(f32[4,64,512]{2,0,1:T(4,128)S(1)} %fusion.18, f32[]{:T(128)} %bitcast.1, f32[8,4,8,512]{3,2,1,0:T(8,128)S(1)} %bitcast.76, bf16[10,512,512]{2,1,0:T(8,128)(2,1)} %param.10), kind=kOutput, calls=%fused_computation.21 | convolution fusion | flops 805568512 | bytes 3670528 | tf_op jit(solution)/shard_map/crk,rqk->crq/dot_general | solution.py:74
  123.4 19.5 %all-reduce = (f32[64]{0:T(128)S(1)}, f32[64]{0:T(128)S(1)}) all-reduce(f32[64]{0:T(128)S(1)} %get-tuple-element.4, f32[64]{0:T(128)S(1)} %get-tuple-element.3), channel_id=1, replica_groups=mesh['ind'=8,'var'=4] {'ind'}, use_global_device_ids=true, to_apply=%region_1.2 | all-reduce | flops 128 | bytes 1024 | tf_op jit(solution)/shard_map/psum | solution.py:60
  143.8 17.1 %psum.37 = f32[64]{0:T(128)S(1)} all-reduce(f32[64]{0:T(128)S(1)} %multiply_reduce_fusion.1), channel_id=1, replica_groups=mesh['ind'=8,'var'=4] {'ind'}, use_global_device_ids=true, to_apply=%region_5.7 | all-reduce | flops 64 | bytes 512 | tf_op jit(solution)/shard_map/psum | solution.py:95
  161.8 2.0 gather_fusion.2
  163.9 45.8 %all_to_all.10 = f32[64,8,2,512]{3,0,2,1:T(8,128)} all-to-all(f32[64,8,2,512]{3,0,2,1:T(8,128)} %bitcast.69), channel_id=1, replica_groups=mesh['ind'=8,'var'=4] {'ind'}, dimensions={1} | all-to-all | bytes 4194304 | tf_op jit(solution)/shard_map/all_to_all | solution.py:68
  209.7 2.2 gather_fusion.4
  211.9 4.9 %fusion.9 = f32[64,6,512]{2,0,1:T(8,128)S(1)} fusion(bf16[10,512,512]{2,1,0:T(8,128)(2,1)} %param.10, f32[6,64,512]{2,1,0:T(8,128)S(1)} %gather_fusion.4, pred[6]{0:T(512)(128)(4,1)S(1)} %get-tuple-element.7), kind=kOutput, calls=%fused_computation.15 | convolution fusion | flops 1208156160 | bytes 4718598 | tf_op jit(solution)/shard_map/csk,sqk->csq/dot_general | solution.py:81
  216.7 1.4 fusion.16
  218.2 4.3 %fusion.13 = f32[4,8,8,512]{3,2,1,0:T(8,128)S(1)} fusion(f32[4,64,512]{2,0,1:T(4,128)S(1)} %fusion.16, f32[]{:T(128)} %bitcast.1, f32[8,4,8,512]{3,2,1,0:T(8,128)S(1)} %bitcast.65, bf16[10,512,512]{2,1,0:T(8,128)(2,1)} %param.10), kind=kOutput, calls=%fused_computation.18 | convolution fusion | flops 805568512 | bytes 3670528 | tf_op jit(solution)/shard_map/crk,rqk->crq/dot_general | solution.py:74
  223.3 19.6 %psum.38 = f32[64]{0:T(128)S(1)} all-reduce(f32[64]{0:T(128)S(1)} %multiply_reduce_fusion), channel_id=1, replica_groups=mesh['ind'=8,'var'=4] {'ind'}, use_global_device_ids=true, to_apply=%region_7.9 | all-reduce | flops 64 | bytes 512 | tf_op jit(solution)/shard_map/psum | solution.py:90
  243.2 1.9 collective-permute-done
  246.4 1.6 collective-permute-start.1
  248.0 23.8 %collective-permute-done.1 = f32[2,64,2048]{2,1,0:T(8,128)S(1)} collective-permute-done((f32[2,64,2048]{2,1,0:T(8,128)}, f32[2,64,2048]{2,1,0:T(8,128)S(1)}, u32[]{:S(2)}, u32[]{:S(2)}) %collective-permute-start.1) | collective-permute-done | bytes 1048608 | tf_op jit(solution)/shard_map/ppermute | solution.py:26
  272.2 9.7 %fusion.4 = f32[64,1,4]{2,1,0:T(1,128)S(1)} fusion(f32[4,64,2048]{2,1,0:T(8,128)S(1)} %bitcast.78, f32[64,2048,1]{1,0,2:T(8,128)S(1)} %bitcast.63), kind=kOutput, calls=%fused_computation.11 | convolution fusion | flops 6291456 | bytes 2622464 | tf_op jit(solution)/shard_map/jn,bjn->jb/dot_general | solution.py:103
  282.0 17.1 %psum.39 = f32[64,4]{0,1:T(4,128)S(1)} all-reduce(f32[64,4]{0,1:T(4,128)S(1)} %bitcast.89), channel_id=1, replica_groups=mesh['ind'=8,'var'=4] {'ind'}, use_global_device_ids=true, to_apply=%region_8.10 | all-reduce | flops 256 | bytes 2048 | tf_op jit(solution)/shard_map/psum | solution.py:104
  (43 shorter events, 8.6 us)
Async XLA Ops:
  0.7 1.6 slice-start
  2.2 41.5 %copy-start.2 = (f32[2]{0:T(128)S(1)}, f32[2]{0:T(128)}, u32[]{:S(2)}) copy-start(f32[2]{0:T(128)} %param.9) | copy-start | bytes 28
  2.3 50.0 %copy-start = (f32[64,2048]{1,0:T(8,128)S(1)}, f32[64,2048]{1,0:T(8,128)}, u32[]{:S(2)}) copy-start(f32[64,2048]{1,0:T(8,128)} %param.8) | copy-start | bytes 1572868
  54.5 8.1 %copy-start.4 = (s32[10]{0:T(128)S(1)}, s32[10]{0:T(128)}, u32[]{:S(2)}) copy-start(s32[10]{0:T(128)} %param.11) | copy-start | bytes 124
  54.5 8.2 %copy-start.3 = (s32[10]{0:T(128)S(1)}, s32[10]{0:T(128)}, u32[]{:S(2)}) copy-start(s32[10]{0:T(128)} %param.12) | copy-start | bytes 124
  54.5 55.7 %all-to-all-start = ((f32[64,8,2,512]{3,0,2,1:T(8,128)}), f32[64,8,2,512]{3,0,2,1:T(8,128)S(1)}, u32[]{:S(2)}, u32[]{:S(2)}) async-start(f32[64,8,2,512]{3,0,2,1:T(8,128)} %bitcast.68), calls=%async_computation | async-start | bytes 4194304 | tf_op jit(solution)/shard_map/all_to_all | solution.py:68
  243.1 3.3 %copy-start.1 = (f32[64,2048]{1,0:T(8,128)}, f32[64,2048]{1,0:T(8,128)S(1)}, u32[]{:S(2)}) copy-start(f32[64,2048]{1,0:T(8,128)S(1)} %multiply_add_fusion) | copy-start | bytes 1572868
  243.1 2.0 collective-permute-start
  246.4 25.4 %collective-permute-start.1 = (f32[2,64,2048]{2,1,0:T(8,128)}, f32[2,64,2048]{2,1,0:T(8,128)S(1)}, u32[]{:S(2)}, u32[]{:S(2)}) collective-permute-start(f32[2,64,2048]{2,1,0:T(8,128)} %get-tuple-element.10), channel_id=1, source_target_pairs={{0,2},{1,3},{2,0},{3,1},{4,6},{5,7},{6,4},{7,5},{8,10},{9,11},{10,... | collective-permute-start | bytes 3145736 | tf_op jit(solution)/shard_map/ppermute | solution.py:26
